TPU v7x, 512 devices: a whole 4x8x8 slice. The times are simulated.
512 devices in a mesh: dp: 16 (over y, core), cell: 32 (over x, z).
Axes of the slice: x: 4, y: 8, z: 8, core: 2. Of those that a mesh axis runs over, the one named last changes fastest.
Arguments:
- sensitivity: bfloat16 [2048, 200704], P('dp', 'cell'), may hold values from -0.0390625 to 0.0390625
- direction: bfloat16 [16, 200704], P(None, 'cell'), may hold values from -6 to 6
- depth_weight: float32 [200704], P('cell'), may hold values from 0.3 to 3
- counts: int32 [32], P('cell'), may hold values from 4704 to 6272, as said below
- send_lists: int32 [32, 2, 128], P('cell'), may hold values from 0 to 6271, as said below
- neighbours: int32 [6, 200704], P(None, 'cell'), may hold values from 0 to 6528, as said below
Outputs:
- product: float32 [16, 200704], P(None, 'cell')
Inputs may be any that keep to these rules, and one draw needn't show every extreme that they name: `counts`: every partition has at least 4704 live cells; some partition is full in every draw. `send_lists`: entries are local indices of live cells of their own partition. `neighbours`: entries below 6272 are live local cells that differ from the cell's own local index by at most 64; 6272 to 6527 name received rim cells; 6528 is an absent face; padded slots hold only absent faces.
All inputs are finite; a program needn't handle non-finite values.
Results may differ from a plain program's by a relative error of at most 0.0008.
Values sent between devices are 32-bit elements; how exact they have to be, the bound alone decides.
No kernel may reach another device: no remote copies, remote signals or barrier semaphores. Data moves between devices by JAX's collectives and lax.ppermute only.
A program may use at most 64 MiB of HBM per device.

v0:
```python
import jax
import jax.numpy as jnp
from jax import lax
from jax.sharding import PartitionSpec as P


def padded_2(value, sides, width):
    for axis, dim in sides:
        count, length = (lax.axis_size(axis), value.shape[dim])
        up = [(i, (i + 1) % count) for i in range(count - 1)]
        down = [(j, i) for i, j in up]
        last = lax.slice_in_dim(value, length - width, length, axis=dim)
        leading = lax.slice_in_dim(value, 0, width, axis=dim)
        before = lax.ppermute(last, axis, up)
        after = lax.ppermute(leading, axis, down)
        value = jnp.concatenate([before, value, after], axis=dim)
    return value


def pick_block():
    block_len = 8
    for candidate in range(128, 7, -8):
        block_len = candidate
        break
    return block_len


def pick_group(block_count):
    group_len = 1
    for candidate in range(1, 9):
        if block_count % candidate == 0:
            group_len = candidate
    return group_len


def smoothness(masked_f, weight, send_lists, neighbours, width):
    slots = masked_f.shape[1]
    values = jnp.concatenate([masked_f * weight[None, :], weight[None, :]], axis=0)
    picked = jnp.take(values, send_lists[0].reshape(-1), axis=1)
    rim = picked.shape[1] // 2
    padded = padded_2(picked, (("cell", 1),), rim)
    rim_vals = jnp.concatenate([padded[:, :rim], padded[:, 3 * rim :]], axis=1)
    lanes = values.shape[0]
    block_len = pick_block()
    block_count = width // block_len
    pieces = 1 + (128 + block_len - 1) // block_len
    spread = jnp.pad(values, ((0, 0), (64, pieces * block_len)))
    local_vals = lax.slice_in_dim(spread, 0, (block_count + pieces - 1) * block_len, axis=1)
    shifted = [
        local_vals[:, m * block_len : (m + block_count) * block_len].reshape(
            lanes, block_count, block_len
        )
        for m in range(pieces)
    ]
    rim_part = jnp.broadcast_to(rim_vals[:, None, :], (lanes, block_count, 2 * rim))
    windows = jnp.concatenate(shifted + [rim_part], axis=2).transpose(1, 0, 2)
    span = windows.shape[2]
    position = jnp.arange(width, dtype=jnp.int32)
    anchor = position // block_len * block_len
    column = jnp.where(
        neighbours < slots,
        neighbours - anchor[None, :] + 64,
        jnp.where(neighbours < slots + 2 * rim, pieces * block_len + neighbours - slots, -1),
    )
    column = column.reshape(neighbours.shape[0], block_count, block_len).transpose(1, 0, 2)
    group_len = pick_group(block_count)
    windows = windows.reshape(block_count // group_len, group_len, lanes, span)
    column = column.reshape(block_count // group_len, group_len, neighbours.shape[0], block_len)

    def gather_block(item):
        window_set, column_set = item
        target = jnp.arange(span, dtype=jnp.int32)[None, None, :, None]
        hits = jnp.sum((column_set[:, :, None, :] == target).astype(jnp.float32), axis=1)
        return jnp.einsum("grw,gwb->grb", window_set, hits, precision=lax.Precision.HIGHEST)

    sums = lax.map(gather_block, (windows, column))
    sums = sums.reshape(block_count, lanes, block_len).transpose(1, 0, 2).reshape(lanes, width)
    coupling = masked_f * sums[-1][None, :] - sums[:-1]
    return weight[None] * weight[None] * masked_f + weight[None] * coupling


def on_device(sensitivity, direction, depth_weight, counts, send_lists, neighbours):
    slots = sensitivity.shape[1]
    nvecs = direction.shape[0]
    live = jnp.arange(slots, dtype=jnp.int32) < counts[0]
    masked = jnp.where(live[None, :], direction, jnp.zeros_like(direction))
    partial_data = lax.dot_general(
        masked, sensitivity, (((1,), (1,)), ((), ())), preferred_element_type=jnp.float32
    )
    summed = lax.psum(partial_data, "cell")
    rounded = summed.astype(jnp.bfloat16)
    remainder = (summed - rounded.astype(jnp.float32)).astype(jnp.bfloat16)
    stacked = jnp.concatenate([rounded, remainder], axis=0)
    both = jnp.dot(stacked, sensitivity, preferred_element_type=jnp.float32)
    partial_cells = both[:nvecs] + both[nvecs:]
    weight = jnp.where(live, depth_weight, jnp.float32(0.0))
    masked_f = masked.astype(jnp.float32)
    misfit = lax.psum(partial_cells, "dp")
    smooth = smoothness(masked_f, weight, send_lists, neighbours, slots)
    total = misfit + 0.5 * smooth
    return jnp.where(live[None, :], total, jnp.float32(0.0))


def solution(mesh):
    placed = (
        P("dp", "cell"),
        P(None, "cell"),
        P("cell"),
        P("cell"),
        P("cell", None, None),
        P(None, "cell"),
    )
    return jax.shard_map(
        on_device, mesh=mesh, in_specs=placed, out_specs=P(None, "cell"), check_vma=False
    )
```

profile of v0, /device:TPU:1, one launch (start us, length us, event | category | flops | bytes accessed | tf_op | source)
XLA Modules:
  0.0 220.8 jit_solution(9854497497350042663)
XLA Ops:
  6.5 0.0 copy-start
  6.5 0.0 all-reduce.3.cloned.1.call-start
  7.3 0.8 fusion.22
  8.1 1.0 convert_multiply_fusion.1
  9.1 0.0 copy-start.5
  9.1 0.1 pad_maximum_fusion.1
  9.2 0.0 copy-start.1
  9.2 2.3 %copy.26 = f32[17,6272]{0,1:T(8,128)} copy(f32[17,6272]{1,0:T(8,128)S(1)} %pad_maximum_fusion.1) | data formatting | bytes 852992 | tf_op jit(solution)/shard_map/concatenate | solution.py:38
  11.5 0.0 copy-done.5
  11.6 2.6 %gather_fusion = f32[256,17]{1,0:T(8,128)S(1)} fusion(f32[17,6272]{0,1:T(8,128)} %copy.26, s32[1024]{0:T(1024)S(1)} %pad_clamp_fusion), kind=kCustom, calls=%fused_computation | custom fusion | bytes 35840 | tf_op jit(solution)/shard_map/jit(_take)/gather | solution.py:39
  14.2 0.1 select_bitcast_fusion
  14.3 0.7 fusion.23
  14.9 5.4 %collective-permute-start = (f32[17,128]{0,1:T(8,128)}, f32[17,128]{0,1:T(8,128)}, u32[]{:S(2)}, u32[]{:S(2)}) collective-permute-start(f32[17,128]{0,1:T(8,128)} %get-tuple-element.42), channel_id=1, source_target_pairs={{0,1},{1,2},{2,3},{3,4},{4,5},{5,6},{6,7},{7,8},{8,9},{9,10},{10,1... | collective-permute-start | bytes 26120 | tf_op jit(solution)/shard_map/ppermute | solution.py:14
  20.4 1.3 collective-permute-start.1
  21.6 0.0 copy-done
  21.7 0.0 copy-done.1
  21.7 0.5 fusion.10
  22.2 0.0 copy-start.4
  22.2 67.6 %psum.14 = f32[16,128]{1,0:T(8,128)S(1)} all-reduce(f32[16,128]{1,0:T(8,128)S(1)} %fusion.10), channel_id=1, replica_groups=mesh['dp'=16,'cell'=32] {'cell'}, use_global_device_ids=true, to_apply=%region_0.1 | all-reduce | flops 2048 | bytes 16384 | tf_op jit(solution)/shard_map/psum | solution.py:90
  89.8 0.4 fusion.16
  90.1 0.8 slice_add_fusion
  90.9 0.0 all-reduce.3.cloned.1.call-update
  91.0 0.0 copy-done.4
  91.0 0.7 select_select_fusion
  91.7 0.4 pad_slice_fusion.1
  92.1 0.8 reshape.80
  92.9 1.1 copy.29
  94.1 0.1 reshape.81
  94.1 0.1 copy.30
  94.2 0.0 collective-permute-done
  94.2 0.9 copy.27
  95.2 0.0 collective-permute-done.1
  95.2 0.1 copy.28
  95.3 0.1 broadcast_in_dim.71
  95.4 0.0 copy-start.3
  95.4 1.7 pad_maximum_fusion
  97.1 0.0 copy-done.3
  97.1 0.0 copy-start.2
  97.1 30.0 %while.10 = (s32[]{:T(128)}, f32[7,7,17,128]{3,2,1,0:T(8,128)S(1)}, f32[7,7,17,512]{3,2,1,0:T(8,128)}, s32[7,7,6,128]{3,2,1,0:T(8,128)}, s32[]{:T(128)}) while((s32[]{:T(128)}, f32[7,7,17,128]{3,2,1,0:T(8,128)S(1)}, f32[7,7,17,512]{3,2,1,0:T(8,128)}, s32[7,7,6,128]{3,2,1,0:T(8,128)}, s32[]{:T(128)}) %tuple.29), condition=%wide.region_4.5_spmd, body=%wide.region_2.4_spmd.sunk | while | flops 101384192 | bytes 4165697 | solution.py:76
  97.1 0.8 dynamic-slice_bitcast_fusion.2
  97.9 1.5 convert_reduce_fusion.2
  99.4 2.0 fusion.32
  101.4 0.8 dynamic-slice_bitcast_fusion.2
  102.2 1.5 convert_reduce_fusion.2
  103.7 2.0 fusion.32
  105.7 0.8 dynamic-slice_bitcast_fusion.2
  106.5 1.5 convert_reduce_fusion.2
  107.9 2.0 fusion.32
  110.0 0.8 dynamic-slice_bitcast_fusion.2
  110.8 1.5 convert_reduce_fusion.2
  112.2 2.0 fusion.32
  114.3 0.8 dynamic-slice_bitcast_fusion.2
  115.0 1.5 convert_reduce_fusion.2
  116.5 2.0 fusion.32
  118.6 0.8 dynamic-slice_bitcast_fusion.2
  119.3 1.5 convert_reduce_fusion.2
  120.8 2.0 fusion.32
  122.8 0.8 dynamic-slice_bitcast_fusion.2
  123.6 1.5 convert_reduce_fusion.2
  125.1 2.0 fusion.32
  127.1 0.1 copy.36
  127.3 84.8 %all-reduce.3.cloned.1.call-done = f32[16,6272]{1,0:T(8,128)} async-done(((f32[16,6272]{1,0:T(8,128)}), f32[16,6272]{1,0:T(8,128)}) %all-reduce.3.cloned.1.call-update) | async-done | bytes 401424 | tf_op jit(solution)/shard_map/psum | solution.py:98
  212.1 0.0 copy-done.2
  212.1 1.9 fusion.7
  (11 shorter events, 0.1 us)
Async XLA Ops:
  6.5 15.1 %copy-start = (bf16[128,6272]{1,0:T(8,128)(2,1)S(1)}, bf16[128,6272]{1,0:T(8,128)(2,1)}, u32[]{:S(2)}) copy-start(bf16[128,6272]{1,0:T(8,128)(2,1)} %param.8) | copy-start | bytes 4816900
  6.5 205.5 %all-reduce.3.cloned.1.call-start = ((), (), s32[]{:S(2)}) async-start(), calls=%async_computation | async-start | bytes 802816 | tf_op jit(solution)/shard_map/psum | solution.py:98
  9.1 2.4 %copy-start.5 = (s32[1,2,128]{2,1,0:T(2,128)S(1)}, s32[1,2,128]{2,1,0:T(2,128)}, u32[]{:S(2)}) copy-start(s32[1,2,128]{2,1,0:T(2,128)} %param.12) | copy-start | bytes 3076
  9.2 12.5 %copy-start.1 = (bf16[16,6272]{1,0:T(8,128)(2,1)S(1)}, bf16[16,6272]{1,0:T(8,128)(2,1)}, u32[]{:S(2)}) copy-start(bf16[16,6272]{1,0:T(8,128)(2,1)} %param.9) | copy-start | bytes 602116
  14.9 79.3 %collective-permute-start = (f32[17,128]{0,1:T(8,128)}, f32[17,128]{0,1:T(8,128)}, u32[]{:S(2)}, u32[]{:S(2)}) collective-permute-start(f32[17,128]{0,1:T(8,128)} %get-tuple-element.42), channel_id=1, source_target_pairs={{0,1},{1,2},{2,3},{3,4},{4,5},{5,6},{6,7},{7,8},{8,9},{9,10},{10,1... | collective-permute-start | bytes 26120 | tf_op jit(solution)/shard_map/ppermute | solution.py:14
  20.4 74.8 %collective-permute-start.1 = (f32[17,128]{0,1:T(8,128)}, f32[17,128]{0,1:T(8,128)S(1)}, u32[]{:S(2)}, u32[]{:S(2)}) collective-permute-start(f32[17,128]{0,1:T(8,128)} %get-tuple-element.43), channel_id=1, source_target_pairs={{1,0},{2,1},{3,2},{4,3},{5,4},{6,5},{7,6},{8,7},{9,8},{10,9},{11,1... | collective-permute-start | bytes 26120 | tf_op jit(solution)/shard_map/ppermute | solution.py:15
  22.2 68.8 %copy-start.4 = (s32[6,6272]{1,0:T(8,128)S(1)}, s32[6,6272]{1,0:T(8,128)}, u32[]{:S(2)}) copy-start(s32[6,6272]{1,0:T(8,128)} %param.13) | copy-start | bytes 451588
  95.4 1.8 copy-start.3
  97.1 115.0 %copy-start.2 = (bf16[16,6272]{1,0:T(8,128)(2,1)S(1)}, bf16[16,6272]{1,0:T(8,128)(2,1)}, u32[]{:S(2)}) copy-start(bf16[16,6272]{1,0:T(8,128)(2,1)} %param.9) | copy-start | bytes 602116
Sparse Core Ops, SparseCore 0:
  91.1 120.9 all-reduce.2
where the time goes:
time: 222 us; the launch traced here: 221 us
  waiting for transfers between devices  84.8 us (38%)
  blocking collectives  67.6 us (30%)
  other arithmetic  17.4 us (8%)
  matrix products  15 us (7%)
  local copies, waits for them, and re-layouts  14.7 us (7%)
  between operations  14.4 us (6%)
  starting transfers between devices  6.7 us (3%)
    psum x1, waiting for transfers between devices, on_device(): misfit = lax.psum(partial_cells, 'dp')  84.8 us
    psum x1, blocking collectives, on_device(): summed = lax.psum(partial_data, 'cell')  67.6 us
    dot_general x7, matrix products, gather_block(): jnp.einsum('grw,gwb->grb', window_set, hits, precision=lax.Precision.HIGH...  14.2 us
    reduce_sum x7, other arithmetic, gather_block(): jnp.sum((column_set[:, :, None, :] == target).astype(jnp.float32), axis=1)  10.3 us
    ppermute x1, starting transfers between devices, padded_2(): before = lax.ppermute(last, axis, up)  5.42 us
    eq x7, local copies, waits for them, and re-layouts, gather_block(): column_set[:, :, None, :] == target  5.32 us
  transfers between devices with their start and end apart: 3, of which 1 were waited for; matrix products, arithmetic and copies ran while one was open for 17% of the time, Pallas kernels for 0%

commit v1 on v0

--- a/solution.py
+++ b/solution.py
@@ -87,7 +87,9 @@
     partial_data = lax.dot_general(
         masked, sensitivity, (((1,), (1,)), ((), ())), preferred_element_type=jnp.float32
     )
-    summed = lax.psum(partial_data, "cell")
+    summed = partial_data
+    for hop in (1, 2, 4, 8, 16):
+        summed = summed + lax.ppermute(summed, "cell", [(dev, dev ^ hop) for dev in range(32)])
     rounded = summed.astype(jnp.bfloat16)
     remainder = (summed - rounded.astype(jnp.float32)).astype(jnp.bfloat16)
     stacked = jnp.concatenate([rounded, remainder], axis=0)

time: 222 us -> 213 us (0.959)
  blocking collectives: 67.6 us -> 0 us
  waiting for transfers between devices: 84.8 us -> 116 us
  starting transfers between devices: 6.7 us -> 32.5 us
    psum x1 -> x0, blocking collectives: 67.6 us -> none  [on_device(): summed = lax.psum(partial_data, 'cell')]
    psum x1, waiting for transfers between devices: 84.8 us -> 114 us  [on_device(): misfit = lax.psum(partial_cells, 'dp')]
    ppermute x0 -> x5, starting transfers between devices: none -> 28.7 us  [on_device(): lax.ppermute(summed, 'cell', [(dev, dev ^ hop) for dev in range(32)])]
    ppermute x1, starting transfers between devices: 5.42 us -> 2.54 us  [padded_2(): before = lax.ppermute(last, axis, up)]
  transfers between devices with their start and end apart: 3 -> 8, of which waited for: 1 -> 2; matrix products, arithmetic and copies ran while one was open for 17% -> 21% of each run, Pallas kernels for 0% -> 0%
where the time goes in v1:
time: 213 us; the launch traced here: 212 us
  waiting for transfers between devices  116 us (54%)
  starting transfers between devices  32.5 us (15%)
  other arithmetic  18.2 us (9%)
  matrix products  15.9 us (7%)
  local copies, waits for them, and re-layouts  15.3 us (7%)
  between operations  14.4 us (7%)
    psum x1, waiting for transfers between devices, on_device(): misfit = lax.psum(partial_cells, 'dp')  114 us
    ppermute x5, starting transfers between devices, on_device(): lax.ppermute(summed, 'cell', [(dev, dev ^ hop) for dev in range(32)])  28.7 us
    dot_general x7, matrix products, gather_block(): jnp.einsum('grw,gwb->grb', window_set, hits, precision=lax.Precision.HIGH...  14.2 us
    reduce_sum x7, other arithmetic, gather_block(): jnp.sum((column_set[:, :, None, :] == target).astype(jnp.float32), axis=1)  10.3 us
    eq x7, local copies, waits for them, and re-layouts, gather_block(): column_set[:, :, None, :] == target  5.28 us
  transfers between devices with their start and end apart: 8, of which 2 were waited for; matrix products, arithmetic and copies ran while one was open for 21% of the time, Pallas kernels for 0%

profile of v1, /device:TPU:1, one launch (start us, length us, event | category | flops | bytes accessed | tf_op | source)
XLA Modules:
  0.0 212.1 jit_solution(7319139454436700179)
XLA Ops:
  7.3 0.6 copy-done
  8.0 1.4 fusion.10
  9.4 4.9 %collective-permute-start = (f32[16,128]{1,0:T(8,128)S(1)}, f32[16,128]{1,0:T(8,128)S(1)}, u32[]{:S(2)}, u32[]{:S(2)}) collective-permute-start(f32[16,128]{1,0:T(8,128)S(1)} %fusion.10), channel_id=1, source_target_pairs={{0,1},{1,0},{2,3},{3,2},{4,5},{5,4},{6,7},{7,6},{8,9},{9,8},{10,11... | collective-permute-start | bytes 24584 | tf_op jit(solution)/shard_map/ppermute | solution.py:92
  14.3 0.8 fusion.22
  15.0 1.0 convert_multiply_fusion.1
  16.0 0.0 copy-start.4
  16.1 0.1 pad_maximum_fusion.1
  16.1 0.0 copy-start.3
  16.1 2.3 %copy.26 = f32[17,6272]{0,1:T(8,128)} copy(f32[17,6272]{1,0:T(8,128)S(1)} %pad_maximum_fusion.1) | data formatting | bytes 852992 | tf_op jit(solution)/shard_map/concatenate | solution.py:38
  18.5 2.6 %gather_fusion = f32[256,17]{1,0:T(8,128)S(1)} fusion(f32[17,6272]{0,1:T(8,128)} %copy.26, s32[1024]{0:T(1024)S(1)} %pad_clamp_fusion), kind=kCustom, calls=%fused_computation | custom fusion | bytes 35840 | tf_op jit(solution)/shard_map/jit(_take)/gather | solution.py:39
  21.1 0.1 select_bitcast_fusion
  21.2 0.7 fusion.23
  21.9 2.5 %collective-permute-start.5 = (f32[17,128]{0,1:T(8,128)}, f32[17,128]{0,1:T(8,128)}, u32[]{:S(2)}, u32[]{:S(2)}) collective-permute-start(f32[17,128]{0,1:T(8,128)} %get-tuple-element.40), channel_id=1, source_target_pairs={{0,1},{1,2},{2,3},{3,4},{4,5},{5,6},{6,7},{7,8},{8,9},{9,10},{10,1... | collective-permute-start | bytes 26120 | tf_op jit(solution)/shard_map/ppermute | solution.py:14
  24.4 1.3 collective-permute-start.6
  25.7 0.7 select_select_fusion
  26.5 0.0 collective-permute-done
  26.5 7.3 %collective-permute-start.1 = (f32[16,128]{1,0:T(8,128)S(1)}, f32[16,128]{1,0:T(8,128)}, u32[]{:S(2)}, u32[]{:S(2)}) collective-permute-start(f32[16,128]{1,0:T(8,128)S(1)} %add.68), channel_id=1, source_target_pairs={{0,2},{1,3},{2,0},{3,1},{4,6},{5,7},{6,4},{7,5},{8,10},{9,11},{10,... | collective-permute-start | bytes 24584 | tf_op jit(solution)/shard_map/ppermute | solution.py:92
  33.7 0.4 pad_slice_fusion.1
  34.1 0.9 reshape.80
  35.0 1.1 copy.29
  36.1 0.1 reshape.81
  36.2 0.1 copy.30
  36.3 0.0 collective-permute-done.5
  36.3 0.9 copy.27
  37.2 0.0 collective-permute-done.6
  37.2 0.1 copy.28
  37.3 0.0 collective-permute-done.1
  37.3 0.7 add.69
  38.0 7.9 %collective-permute-start.2 = (f32[16,128]{1,0:T(8,128)S(1)}, f32[16,128]{1,0:T(8,128)S(1)}, u32[]{:S(2)}, u32[]{:S(2)}) collective-permute-start(f32[16,128]{1,0:T(8,128)S(1)} %add.69), channel_id=1, source_target_pairs={{0,4},{1,5},{2,6},{3,7},{4,0},{5,1},{6,2},{7,3},{8,12},{9,13},{10,... | collective-permute-start | bytes 24584 | tf_op jit(solution)/shard_map/ppermute | solution.py:92
  46.0 1.0 collective-permute-done.2
  47.0 4.0 %collective-permute-start.3 = (f32[16,128]{1,0:T(8,128)S(1)}, f32[16,128]{1,0:T(8,128)S(1)}, u32[]{:S(2)}, u32[]{:S(2)}) collective-permute-start(f32[16,128]{1,0:T(8,128)S(1)} %add.70), channel_id=1, source_target_pairs={{0,8},{1,9},{2,10},{3,11},{4,12},{5,13},{6,14},{7,15},{8,0},{9,1},... | collective-permute-start | bytes 24584 | tf_op jit(solution)/shard_map/ppermute | solution.py:92
  51.0 0.1 broadcast_in_dim.71
  51.1 1.8 pad_maximum_fusion
  52.9 0.0 collective-permute-done.3
  52.9 4.6 %collective-permute-start.4 = (f32[16,128]{1,0:T(8,128)S(1)}, f32[16,128]{1,0:T(8,128)S(1)}, u32[]{:S(2)}, u32[]{:S(2)}) collective-permute-start(f32[16,128]{1,0:T(8,128)S(1)} %add.71), channel_id=1, source_target_pairs={{0,16},{1,17},{2,18},{3,19},{4,20},{5,21},{6,22},{7,23},{8,24},{9,... | collective-permute-start | bytes 24584 | tf_op jit(solution)/shard_map/ppermute | solution.py:92
  57.5 30.0 %while.10 = (s32[]{:T(128)}, f32[7,7,17,128]{3,2,1,0:T(8,128)S(1)}, f32[7,7,17,512]{3,2,1,0:T(8,128)}, s32[7,7,6,128]{3,2,1,0:T(8,128)}, s32[]{:T(128)}) while((s32[]{:T(128)}, f32[7,7,17,128]{3,2,1,0:T(8,128)S(1)}, f32[7,7,17,512]{3,2,1,0:T(8,128)}, s32[7,7,6,128]{3,2,1,0:T(8,128)}, s32[]{:T(128)}) %tuple.29), condition=%wide.region_3.4_spmd, body=%wide.region_1.3_spmd.sunk | while | flops 101384192 | bytes 4165697 | solution.py:76
  57.5 0.8 dynamic-slice_bitcast_fusion.2
  58.3 1.5 convert_reduce_fusion.2
  59.8 2.0 fusion.32
  61.8 0.8 dynamic-slice_bitcast_fusion.2
  62.6 1.5 convert_reduce_fusion.2
  64.1 2.0 fusion.32
  66.1 0.8 dynamic-slice_bitcast_fusion.2
  66.9 1.5 convert_reduce_fusion.2
  68.3 2.0 fusion.32
  70.4 0.8 dynamic-slice_bitcast_fusion.2
  71.1 1.5 convert_reduce_fusion.2
  72.6 2.0 fusion.32
  74.7 0.8 dynamic-slice_bitcast_fusion.2
  75.4 1.5 convert_reduce_fusion.2
  76.9 2.0 fusion.32
  79.0 0.8 dynamic-slice_bitcast_fusion.2
  79.7 1.5 convert_reduce_fusion.2
  81.2 2.0 fusion.32
  83.2 0.8 dynamic-slice_bitcast_fusion.2
  84.0 1.5 convert_reduce_fusion.2
  85.5 2.0 fusion.32
  87.5 0.1 copy.36
  87.6 0.0 copy-start.1
  87.7 0.4 fusion.16
  88.0 0.8 slice_add_fusion
  88.8 0.0 all-reduce.3.cloned.1.call-update
  88.9 114.5 %all-reduce.3.cloned.1.call-done = f32[16,6272]{1,0:T(8,128)} async-done(((f32[16,6272]{1,0:T(8,128)}), f32[16,6272]{1,0:T(8,128)}) %all-reduce.3.cloned.1.call-update) | async-done | bytes 401424 | tf_op jit(solution)/shard_map/psum | solution.py:100
  203.4 1.9 fusion.7
  (22 shorter events, 0.1 us)
Async XLA Ops:
  6.5 1.4 copy-start
  6.5 196.8 %all-reduce.3.cloned.1.call-start = ((), (), s32[]{:S(2)}) async-start(), calls=%async_computation | async-start | bytes 802816 | tf_op jit(solution)/shard_map/psum | solution.py:100
  9.4 17.1 %collective-permute-start = (f32[16,128]{1,0:T(8,128)S(1)}, f32[16,128]{1,0:T(8,128)S(1)}, u32[]{:S(2)}, u32[]{:S(2)}) collective-permute-start(f32[16,128]{1,0:T(8,128)S(1)} %fusion.10), channel_id=1, source_target_pairs={{0,1},{1,0},{2,3},{3,2},{4,5},{5,4},{6,7},{7,6},{8,9},{9,8},{10,11... | collective-permute-start | bytes 24584 | tf_op jit(solution)/shard_map/ppermute | solution.py:92
  16.0 2.4 %copy-start.4 = (s32[1,2,128]{2,1,0:T(2,128)S(1)}, s32[1,2,128]{2,1,0:T(2,128)}, u32[]{:S(2)}) copy-start(s32[1,2,128]{2,1,0:T(2,128)} %param.12) | copy-start | bytes 3076
  16.1 9.6 %copy-start.3 = (s32[6,6272]{1,0:T(8,128)S(1)}, s32[6,6272]{1,0:T(8,128)}, u32[]{:S(2)}) copy-start(s32[6,6272]{1,0:T(8,128)} %param.13) | copy-start | bytes 451588
  21.9 14.4 %collective-permute-start.5 = (f32[17,128]{0,1:T(8,128)}, f32[17,128]{0,1:T(8,128)}, u32[]{:S(2)}, u32[]{:S(2)}) collective-permute-start(f32[17,128]{0,1:T(8,128)} %get-tuple-element.40), channel_id=1, source_target_pairs={{0,1},{1,2},{2,3},{3,4},{4,5},{5,6},{6,7},{7,8},{8,9},{9,10},{10,1... | collective-permute-start | bytes 26120 | tf_op jit(solution)/shard_map/ppermute | solution.py:14
  24.4 12.8 %collective-permute-start.6 = (f32[17,128]{0,1:T(8,128)}, f32[17,128]{0,1:T(8,128)S(1)}, u32[]{:S(2)}, u32[]{:S(2)}) collective-permute-start(f32[17,128]{0,1:T(8,128)} %get-tuple-element.41), channel_id=1, source_target_pairs={{1,0},{2,1},{3,2},{4,3},{5,4},{6,5},{7,6},{8,7},{9,8},{10,9},{11,1... | collective-permute-start | bytes 26120 | tf_op jit(solution)/shard_map/ppermute | solution.py:15
  26.5 10.8 %collective-permute-start.1 = (f32[16,128]{1,0:T(8,128)S(1)}, f32[16,128]{1,0:T(8,128)}, u32[]{:S(2)}, u32[]{:S(2)}) collective-permute-start(f32[16,128]{1,0:T(8,128)S(1)} %add.68), channel_id=1, source_target_pairs={{0,2},{1,3},{2,0},{3,1},{4,6},{5,7},{6,4},{7,5},{8,10},{9,11},{10,... | collective-permute-start | bytes 24584 | tf_op jit(solution)/shard_map/ppermute | solution.py:92
  38.0 9.0 %collective-permute-start.2 = (f32[16,128]{1,0:T(8,128)S(1)}, f32[16,128]{1,0:T(8,128)S(1)}, u32[]{:S(2)}, u32[]{:S(2)}) collective-permute-start(f32[16,128]{1,0:T(8,128)S(1)} %add.69), channel_id=1, source_target_pairs={{0,4},{1,5},{2,6},{3,7},{4,0},{5,1},{6,2},{7,3},{8,12},{9,13},{10,... | collective-permute-start | bytes 24584 | tf_op jit(solution)/shard_map/ppermute | solution.py:92
  47.0 5.9 %collective-permute-start.3 = (f32[16,128]{1,0:T(8,128)S(1)}, f32[16,128]{1,0:T(8,128)S(1)}, u32[]{:S(2)}, u32[]{:S(2)}) collective-permute-start(f32[16,128]{1,0:T(8,128)S(1)} %add.70), channel_id=1, source_target_pairs={{0,8},{1,9},{2,10},{3,11},{4,12},{5,13},{6,14},{7,15},{8,0},{9,1},... | collective-permute-start | bytes 24584 | tf_op jit(solution)/shard_map/ppermute | solution.py:92
  51.1 6.4 %copy-start.2 = (f32[7,7,17,128]{3,2,1,0:T(8,128)S(1)}, f32[7,7,17,128]{3,2,1,0:T(8,128)}, u32[]{:S(2)}) copy-start(f32[7,7,17,128]{3,2,1,0:T(8,128)} %custom-call.2) | copy-start | bytes 1279492
  52.9 34.8 %collective-permute-start.4 = (f32[16,128]{1,0:T(8,128)S(1)}, f32[16,128]{1,0:T(8,128)S(1)}, u32[]{:S(2)}, u32[]{:S(2)}) collective-permute-start(f32[16,128]{1,0:T(8,128)S(1)} %add.71), channel_id=1, source_target_pairs={{0,16},{1,17},{2,18},{3,19},{4,20},{5,21},{6,22},{7,23},{8,24},{9,... | collective-permute-start | bytes 24584 | tf_op jit(solution)/shard_map/ppermute | solution.py:92
  87.6 115.8 %copy-start.1 = (bf16[16,6272]{1,0:T(8,128)(2,1)S(1)}, bf16[16,6272]{1,0:T(8,128)(2,1)}, u32[]{:S(2)}) copy-start(bf16[16,6272]{1,0:T(8,128)(2,1)} %param.9) | copy-start | bytes 602116
Sparse Core Ops, SparseCore 0:
  89.0 114.3 all-reduce.2
